TPU v7x, 128 devices: a whole 4x4x4 slice. The times are simulated.
128 devices in a mesh: chan: 8 (over y_hi, x), tm: 16 (over z, y_lo, core).
Axes of the slice: x: 4, y: 4 (y_hi: 2, y_lo: 2; y = y_hi * 2 + y_lo), z: 4, core: 2. Of those that a mesh axis runs over, the one named last changes fastest.
Arguments:
- traces: bfloat16 [128, 1024, 2048], P('tm', 'chan'), may hold values from -6 to 6
- live: int32 [1024], P('chan'), may hold values 0 or 1
Outputs:
- correlations: bfloat16 [1024, 128, 2048], P(('chan', 'tm'))
Inputs may be any that keep to these rules, and one draw needn't show every extreme that they name: `live`: 1 marks a usable channel, 0 a dead one.
All inputs are finite; a program needn't handle non-finite values. No bound on the sum of `live` on one device may be relied on, other than what follows from the above.
Results may differ from a plain program's by a relative error of at most 0.0076.
Values may be sent and summed in bfloat16 or wider, within the bound.
No kernel may reach another device: no remote copies, remote signals or barrier semaphores. Data moves between devices by JAX's collectives and lax.ppermute only.
A program may use at most 128 MiB of HBM per device.

v0:
```python
import math
import jax
import jax.numpy as jnp
from jax import lax
from jax.sharding import PartitionSpec as P

SMOOTH = 4


def from_behind(block, axis, distance):
    devices = range(lax.axis_size(axis))
    route = [(i - distance, i) for i in devices if i - distance in devices]
    return lax.ppermute(block, axis, route)


def column_bins(count, group_width):
    index = jnp.arange(count, dtype=jnp.int32)
    group = index // (2 * group_width)
    within = index % group_width
    is_imag = index // group_width % 2
    return (group * group_width + within, is_imag)


def forward_table(samples, bins, group_width):
    freq, is_imag = column_bins(2 * bins, group_width)
    moments = jnp.arange(samples, dtype=jnp.int32)[:, None]
    phase = (moments * freq[None, :] % samples).astype(jnp.float32) * (2.0 * math.pi / samples)
    return jnp.where(is_imag[None, :] == 1, -jnp.sin(phase), jnp.cos(phase)).astype(jnp.bfloat16)


def inverse_table(samples, bins, group_width, segments):
    freq, is_imag = column_bins(2 * bins, group_width)
    lag = jnp.arange(samples, dtype=jnp.int32) - samples // 2
    phase = jnp.mod(freq[:, None] * lag[None, :], samples).astype(jnp.float32) * (
        2.0 * math.pi / samples
    )
    weight = jnp.where(freq == 0, 1.0, 2.0).astype(jnp.float32) / math.sqrt(samples * segments)
    wave = jnp.where(is_imag[:, None] == 1, -jnp.sin(phase), jnp.cos(phase))
    return (weight[:, None] * wave).astype(jnp.bfloat16)


def whiten(spectra, groups):
    lead = spectra.shape[:-1]
    bins = spectra.shape[-1] // 2
    width = bins // groups
    split = spectra.reshape(lead + (groups, 2, width))
    real_part = split[..., 0, :].reshape(lead + (bins,))
    imag_part = split[..., 1, :].reshape(lead + (bins,))
    amplitude = jnp.sqrt(real_part * real_part + imag_part * imag_part)
    padded = jnp.pad(amplitude, [(0, 0)] * len(lead) + [(SMOOTH, SMOOTH)])
    smooth = sum((padded[..., i : i + bins] for i in range(2 * SMOOTH + 1))) / (2 * SMOOTH + 1)
    water = 0.8 * jnp.mean(amplitude, axis=-1, keepdims=True) + 1e-06
    level = jnp.maximum(smooth, water).reshape(lead + (groups, 1, width))
    return (split / level).reshape(lead + (2 * bins,)).astype(jnp.bfloat16)


def band(matrix):
    rows, width, extra = matrix.shape
    flat = matrix.reshape(rows * width, extra)
    flat = jnp.pad(flat, ((0, rows), (0, 0)))
    return flat.reshape(rows, width + 1, extra)[:, 1 : rows + 1, :]


def product(left, right):
    return jnp.einsum("sah,sbh->abh", left, right, preferred_element_type=jnp.float32)


def cross(own_white, extended, own_flags, ext_flags, half):
    own_real = own_white[..., :half]
    own_imag = own_white[..., half:]
    ext_real = extended[..., :half]
    ext_imag = extended[..., half:]
    real_sum = product(own_real, ext_real) + product(own_imag, ext_imag)
    imag_sum = product(own_imag, ext_real) - product(own_real, ext_imag)
    pair_flags = band((own_flags[:, None] * ext_flags[None, :])[:, :, None])
    both = jnp.concatenate([band(real_sum), band(imag_sum)], axis=-1)
    return (both * pair_flags).astype(jnp.bfloat16)


def transform_rows(traces_part, table, groups):
    seg_dev, rows, samples = traces_part.shape
    spectra = jnp.dot(
        traces_part.reshape(seg_dev * rows, samples), table, preferred_element_type=jnp.float32
    )
    return whiten(spectra.reshape(seg_dev, rows, table.shape[1]), groups)


def body(traces, live):
    seg_dev, block, samples = traces.shape
    bins = samples // 2
    groups = lax.axis_size("tm")
    group_width = bins // groups
    segments = seg_dev * groups
    table = forward_table(samples, bins, group_width)
    inverse = inverse_table(samples, bins, group_width, segments)
    flags = live.astype(jnp.bfloat16)
    white = transform_rows(traces, table, groups)
    own_white = lax.all_to_all(white, "tm", split_axis=2, concat_axis=0, tiled=True)
    next_white, next_flags = from_behind((own_white, flags), "chan", -1)
    extended = jnp.concatenate([own_white, next_white], axis=1)
    ext_flags = jnp.concatenate([flags, next_flags], axis=0).astype(jnp.float32)
    stack = cross(own_white, extended, flags.astype(jnp.float32), ext_flags, group_width)
    lagged = jnp.einsum(
        "rif,fl->ril",
        lax.all_to_all(stack, "tm", split_axis=0, concat_axis=2, tiled=True),
        inverse,
        preferred_element_type=jnp.float32,
    )
    return lagged.astype(jnp.bfloat16)


def solution(mesh):
    in_specs = (P("tm", "chan", None), P("chan"))
    out_specs = P(("chan", "tm"), None, None)
    return jax.shard_map(body, mesh=mesh, in_specs=in_specs, out_specs=out_specs, check_vma=False)
```

profile of v0, /device:TPU:15, one launch (start us, length us, event | category | flops | bytes accessed | tf_op | source)
XLA Modules:
  0.0 501.4 jit_solution(12452085739045821830)
XLA Ops:
  0.0 0.0 copy-start.3
  0.0 0.6 copy-done.3
  0.6 67.4 %select_convert_fusion.4 = bf16[2048,2048]{1,0:T(8,128)(2,1)S(1)} fusion(s32[2048]{0:T(1024)S(1)} %fusion.52, pred[2048]{0:T(1024)(128)(4,1)S(1)} %fusion.49), kind=kLoop, calls=%fused_computation.15.clone.clone.1 | loop fusion | flops 71303168 | bytes 8398848 | tf_op jit(solution)/shard_map/dot_general | solution.py:82
  68.0 0.0 copy-done.5
  68.0 0.0 copy-done.7
  68.0 11.0 %fusion.12 = f32[2048,1024]{0,1:T(8,128)} fusion(bf16[1024,2048]{1,0:T(8,128)(2,1)S(1)} %bitcast.77, bf16[2048,2048]{1,0:T(8,128)(2,1)S(1)} %select_convert_fusion.4), kind=kOutput, calls=%fused_computation.21 | convolution fusion | flops 8589934592 | bytes 20971520 | tf_op jit(solution)/shard_map/dot_general | solution.py:82
  79.0 9.7 %copy.20 = f32[1024,2048]{0,1:T(8,128)} copy(f32[1024,2048]{1,0:T(8,128)} %bitcast.67) | data formatting | bytes 16777216 | tf_op jit(solution)/shard_map/dot_general | solution.py:82
  88.7 5.5 %copy.39 = f32[256,8,8,128]{3,2,1,0:T(8,128)S(1)} copy(f32[256,8,8,128]{3,1,2,0:T(8,128)} %bitcast.70) | data formatting | bytes 16777216
  94.1 1.5 fusion.63
  95.6 2.8 copy.21
  98.4 9.1 %copy.22 = f32[8,128,2048]{1,2,0:T(8,128)} copy(f32[8,128,2048]{2,1,0:T(8,128)} %bitcast.68) | data formatting | bytes 16777216 | tf_op jit(solution)/shard_map/reshape;reshape | solution.py:46
  107.5 18.4 %multiply_maximum_fusion = f32[8,128,1024]{1,2,0:T(8,128)} fusion(f32[8,128,1024]{1,2,0:T(8,128)} %bitcast.72, f32[8,128]{1,0:T(8,128)S(1)} %multiply_add_fusion), kind=kLoop, calls=%fused_computation.48 | loop fusion | flops 10485760 | bytes 8392704 | tf_op jit(solution)/shard_map/max | solution.py:53
  125.9 0.0 copy-done
  125.9 5.0 %fusion.14 = bf16[8,128,2048]{1,2,0:T(8,128)(2,1)} fusion(f32[8,128,2048]{1,2,0:T(8,128)S(1)} %copy-done, f32[8,128,16,64]{1,3,2,0:T(8,128)} %bitcast.73), kind=kLoop, calls=%fused_computation.26 | loop fusion | flops 4194304 | bytes 16777216 | tf_op jit(solution)/shard_map/convert_element_type | solution.py:54
  131.0 4.9 copy.23
  135.8 0.0 copy-start.8
  135.9 55.9 %all_to_all.36 = bf16[8,128,2048]{1,0,2:T(8,128)(2,1)S(1)} all-to-all(bf16[8,128,2048]{1,0,2:T(8,128)(2,1)S(1)} %copy.23), channel_id=1, replica_groups=mesh['chan'=8,'tm'=16] {'tm'}, dimensions={2} | all-to-all | bytes 8388608 | tf_op jit(solution)/shard_map/all_to_all | solution.py:98
  191.7 3.2 copy.46
  195.0 2.4 collective-permute-start
  197.4 0.0 copy-done.8
  197.4 2.3 collective-permute-start.1
  199.8 92.7 %collective-permute-done.1 = bf16[128]{0:T(256)(128)(2,1)S(1)} collective-permute-done((bf16[128]{0:T(256)(128)(2,1)S(1)}, bf16[128]{0:T(256)(128)(2,1)S(1)}, u32[]{:S(2)}, u32[]{:S(2)}) %collective-permute-start.1) | collective-permute-done | bytes 288 | tf_op jit(solution)/shard_map/ppermute | solution.py:13
  292.5 0.1 multiply_bitcast_fusion
  292.6 0.1 copy.42
  292.8 0.3 pad_reduce_fusion
  293.1 0.3 reshape.177
  293.4 0.7 slice_bitcast_fusion
  294.1 0.0 collective-permute-done
  294.1 4.2 fusion.37
  298.4 7.9 %add_bitcast_fusion = f32[128,256,64]{0,1,2:T(8,128)} fusion(f32[64,256,128]{2,1,0:T(8,128)S(1)} %fusion.37, bf16[128,128,128]{1,0,2:T(8,128)(2,1)} %bitcast.64, bf16[128,128,128]{1,0,2:T(8,128)(2,1)} %collective-permute-done), kind=kOutput, calls=%fused_computation.31 | convolution fusion | flops 555745280 | bytes 27262976 | tf_op jit(solution)/shard_map/sah,sbh->abh/dot_general | solution.py:65
  306.2 9.2 %copy.40 = f32[8,8,128,256]{3,1,2,0:T(8,128)} copy(f32[8,8,128,256]{2,3,1,0:T(8,128)} %bitcast.75) | data formatting | bytes 16777216
  315.4 7.2 %pad.16 = f32[32896,64]{0,1:T(8,128)} pad(f32[32768,64]{0,1:T(8,128)} %bitcast.66, f32[]{:T(128)} %constant.116.clone.1), padding=0_128x0_0 | pad | bytes 16809988 | tf_op jit(solution)/shard_map/jit(_pad)/pad | solution.py:60
  322.6 14.2 %reshape.174 = f32[128,257,64]{1,0,2:T(8,128)} reshape(f32[32896,64]{0,1:T(8,128)} %pad.16) | data formatting | bytes 16842752 | tf_op jit(solution)/shard_map/reshape | solution.py:61
  336.8 6.5 %slice.73 = f32[128,128,64]{1,0,2:T(8,128)} slice(f32[128,257,64]{1,0,2:T(8,128)} %reshape.174), slice={[0:128], [1:129], [0:64]} | slice | bytes 8388608 | tf_op jit(solution)/shard_map/slice | solution.py:61
  343.3 4.2 fusion.39
  347.5 7.9 %subtract_bitcast_fusion = f32[128,256,64]{0,1,2:T(8,128)} fusion(f32[64,256,128]{2,1,0:T(8,128)S(1)} %fusion.39, bf16[128,128,128]{1,0,2:T(8,128)(2,1)} %bitcast.64, bf16[128,128,128]{1,0,2:T(8,128)(2,1)} %collective-permute-done), kind=kOutput, calls=%fused_computation.30 | convolution fusion | flops 555745280 | bytes 27262976 | tf_op jit(solution)/shard_map/sah,sbh->abh/dot_general | solution.py:65
  355.4 9.2 %copy.41 = f32[8,8,128,256]{3,1,2,0:T(8,128)} copy(f32[8,8,128,256]{2,3,1,0:T(8,128)} %bitcast.74) | data formatting | bytes 16777216
  364.6 7.2 %pad.17 = f32[32896,64]{0,1:T(8,128)} pad(f32[32768,64]{0,1:T(8,128)} %bitcast.65, f32[]{:T(128)} %constant.116.clone.1), padding=0_128x0_0 | pad | bytes 16809988 | tf_op jit(solution)/shard_map/jit(_pad)/pad | solution.py:60
  371.7 14.2 %reshape.176 = f32[128,257,64]{1,0,2:T(8,128)} reshape(f32[32896,64]{0,1:T(8,128)} %pad.17) | data formatting | bytes 16842752 | tf_op jit(solution)/shard_map/reshape | solution.py:61
  385.9 4.7 slice.74
  390.6 1.4 fusion.13
  392.0 4.7 copy.31
  396.8 5.5 %all-to-all-start.1 = ((bf16[128,128,128]{1,2,0:T(8,128)(2,1)}), bf16[128,128,128]{1,2,0:T(8,128)(2,1)}, u32[]{:S(2)}, u32[]{:S(2)}) async-start(bf16[128,128,128]{1,2,0:T(8,128)(2,1)} %copy.31), calls=%async_computation.1 | async-start | bytes 8388608 | tf_op jit(solution)/shard_map/all_to_all | solution.py:105
  402.3 71.1 %fusion.72 = bf16[2048,2048,1]{1,0,2:T(8,128)(2,1)} fusion(s32[2048]{0:T(1024)S(1)} %iota_add_fusion, s32[2048]{0:T(1024)S(1)} %copy-done.4, f32[2048]{0:T(1024)S(1)} %select_multiply_fusion, pred[2048]{0:T(1024)(128)(4,1)S(1)} %copy-done.6), kind=kLoop, calls=%fused_computation.19.clone.clone.clone.clone.1 | loop fusion | flops 75497472 | bytes 8415232 | tf_op jit(solution)/shard_map/rif,fl->ril/dot_general | solution.py:103
  473.4 0.0 all-to-all-done.1
  473.4 6.7 %copy.33 = bf16[8,128,16,128]{3,2,1,0:T(8,128)(2,1)} copy(bf16[8,128,16,128]{1,3,0,2:T(8,128)(2,1)} %bitcast.15) | data formatting | bytes 8388608 | tf_op jit(solution)/shard_map/all_to_all | solution.py:105
  480.1 7.3 %all_to_all.33 = bf16[8,128,2048]{2,1,0:T(8,128)(2,1)} reshape(bf16[8,128,16,128]{3,2,1,0:T(8,128)(2,1)} %copy.33) | data formatting | bytes 8388608 | tf_op jit(solution)/shard_map/all_to_all | solution.py:105
  487.4 13.8 %fusion.33 = bf16[8,128,2048]{2,1,0:T(8,128)(2,1)} fusion(bf16[8,128,2048]{2,1,0:T(8,128)(2,1)} %all_to_all.33, bf16[2048,2048,1]{1,0,2:T(8,128)(2,1)} %fusion.72), kind=kOutput, calls=%fused_computation.54 | convolution fusion | flops 8592031744 | bytes 16777216 | tf_op jit(solution)/shard_map/rif,fl->ril/dot_general | solution.py:103
  (18 shorter events, 0.1 us)
Async XLA Ops:
  0.0 68.0 %copy-start.7 = (bf16[8,128,2048]{2,1,0:T(8,128)(2,1)S(1)}, bf16[8,128,2048]{2,1,0:T(8,128)(2,1)}, u32[]{:S(2)}) copy-start(bf16[8,128,2048]{2,1,0:T(8,128)(2,1)} %param.2) | copy-start | bytes 12582916
  0.0 0.6 copy-start.3
  0.6 67.4 %copy-start.5 = (pred[2048]{0:T(1024)(128)(4,1)}, pred[2048]{0:T(1024)(128)(4,1)S(1)}, u32[]{:S(2)}) copy-start(pred[2048]{0:T(1024)(128)(4,1)S(1)} %fusion.49) | copy-start | bytes 6148
  107.5 18.4 %copy-start = (f32[8,128,2048]{1,2,0:T(8,128)S(1)}, f32[8,128,2048]{1,2,0:T(8,128)}, u32[]{:S(2)}) copy-start(f32[8,128,2048]{1,2,0:T(8,128)} %copy.22) | copy-start | bytes 25165828
  135.8 61.6 %copy-start.8 = (s32[128]{0:T(128)S(1)}, s32[128]{0:T(128)}, u32[]{:S(2)}) copy-start(s32[128]{0:T(128)} %param.3) | copy-start | bytes 1540
  195.0 99.2 %collective-permute-start = (bf16[128,128,128]{1,0,2:T(8,128)(2,1)}, bf16[128,128,128]{1,0,2:T(8,128)(2,1)}, u32[]{:S(2)}, u32[]{:S(2)}) collective-permute-start(bf16[128,128,128]{1,0,2:T(8,128)(2,1)} %bitcast.64), channel_id=1, source_target_pairs={{16,0},{32,16},{48,32},{64,48},{80,64},{96,80},{112,96},{17,1},{33... | collective-permute-start | bytes 12582920 | tf_op jit(solution)/shard_map/ppermute | solution.py:13
  197.4 95.1 %collective-permute-start.1 = (bf16[128]{0:T(256)(128)(2,1)S(1)}, bf16[128]{0:T(256)(128)(2,1)S(1)}, u32[]{:S(2)}, u32[]{:S(2)}) collective-permute-start(bf16[128]{0:T(256)(128)(2,1)S(1)} %get-tuple-element.8), channel_id=1, source_target_pairs={{16,0},{32,16},{48,32},{64,48},{80,64},{96,80},{112,96},{17,1},{33... | collective-permute-start | bytes 776 | tf_op jit(solution)/shard_map/ppermute | solution.py:13
  385.9 4.7 copy-start.1
  385.9 4.7 copy-start.2
  392.0 10.2 %copy-start.4 = (s32[2048]{0:T(1024)S(1)}, s32[2048]{0:T(1024)}, u32[]{:S(2)}) copy-start(s32[2048]{0:T(1024)} %copy-done.3) | copy-start | bytes 24580
  392.0 10.2 %copy-start.6 = (pred[2048]{0:T(1024)(128)(4,1)S(1)}, pred[2048]{0:T(1024)(128)(4,1)}, u32[]{:S(2)}) copy-start(pred[2048]{0:T(1024)(128)(4,1)} %copy-done.5) | copy-start | bytes 6148
  396.8 76.6 %all-to-all-start.1 = ((bf16[128,128,128]{1,2,0:T(8,128)(2,1)}), bf16[128,128,128]{1,2,0:T(8,128)(2,1)}, u32[]{:S(2)}, u32[]{:S(2)}) async-start(bf16[128,128,128]{1,2,0:T(8,128)(2,1)} %copy.31), calls=%async_computation.1 | async-start | bytes 8388608 | tf_op jit(solution)/shard_map/all_to_all | solution.py:105
where the time goes:
time: 509 us; the launch traced here: 501 us
  other arithmetic  165 us (32%)
  local copies, waits for them, and re-layouts  128 us (25%)
  waiting for transfers between devices  92.7 us (18%)
  blocking collectives  55.9 us (11%)
  matrix products  49 us (10%)
  starting transfers between devices  10.3 us (2%)
    ppermute x2, waiting for transfers between devices, from_behind(): return lax.ppermute(block, axis, route)  92.7 us
    dot_general x1, other arithmetic, body(): jnp.einsum('rif,fl->ril', lax.all_to_all(stack, 'tm', split_axis=0, conca...  71.1 us
    dot_general x1, other arithmetic, transform_rows(): jnp.dot(traces_part.reshape(seg_dev * rows, samples), table, preferred_el...  67.4 us
    all_to_all x1, blocking collectives, body(): lax.all_to_all(white, 'tm', split_axis=2, concat_axis=0, tiled=True)  55.9 us
    reshape x3, local copies, waits for them, and re-layouts, band(): return flat.reshape(rows, width + 1, extra)[:, 1:rows + 1, :]  28.7 us
    unnamed x22, local copies, waits for them, and re-layouts  24.6 us
    dot_general x4, matrix products, product(): jnp.einsum('sah,sbh->abh', left, right, preferred_element_type=jnp.float32)  24.2 us
    max x1, other arithmetic, whiten(): level = jnp.maximum(smooth, water).reshape(lead + (groups, 1, width))  18.4 us
  transfers between devices with their start and end apart: 3, of which 1 were waited for; matrix products, arithmetic and copies ran while one was open for 14% of the time, Pallas kernels for 0%

commit v1 on v0

--- a/solution.py
+++ b/solution.py
@@ -5,6 +5,12 @@
 from jax.sharding import PartitionSpec as P
 
 SMOOTH = 4
+
+
+def exchange_blocks(block, mesh_axis, split, join):
+    pieces = jnp.split(block, lax.axis_size(mesh_axis), axis=split)
+    got = lax.all_to_all(jnp.stack(pieces), mesh_axis, 0, 0)
+    return jnp.concatenate(got, axis=join)
 
 
 def from_behind(block, axis, distance):
@@ -102,7 +108,7 @@
     stack = cross(own_white, extended, flags.astype(jnp.float32), ext_flags, group_width)
     lagged = jnp.einsum(
         "rif,fl->ril",
-        lax.all_to_all(stack, "tm", split_axis=0, concat_axis=2, tiled=True),
+        exchange_blocks(stack, "tm", 0, 2),
         inverse,
         preferred_element_type=jnp.float32,
     )

time: 509 us -> 503 us (0.988)
  local copies, waits for them, and re-layouts: 128 us -> 121 us
    all_to_all x2 -> x0, local copies, waits for them, and re-layouts: 14 us -> none  [body(): lax.all_to_all(stack, 'tm', split_axis=0, concat_axis=2, tiled=True)]
    unnamed x22 -> x37, local copies, waits for them, and re-layouts: 24.6 us -> 35.7 us
  transfers between devices with their start and end apart: 3 -> 3, of which waited for: 1 -> 1; matrix products, arithmetic and copies ran while one was open for 14% -> 15% of each run, Pallas kernels for 0% -> 0%
where the time goes in v1:
time: 503 us; the launch traced here: 495 us
  other arithmetic  165 us (33%)
  local copies, waits for them, and re-layouts  121 us (24%)
  waiting for transfers between devices  92.9 us (18%)
  blocking collectives  55.9 us (11%)
  matrix products  49.2 us (10%)
  starting transfers between devices  10.6 us (2%)
    ppermute x2, waiting for transfers between devices, from_behind(): return lax.ppermute(block, axis, route)  92.9 us
    dot_general x1, other arithmetic, body(): jnp.einsum('rif,fl->ril', exchange_blocks(stack, 'tm', 0, 2), inverse, pr...  71.1 us
    dot_general x1, other arithmetic, transform_rows(): jnp.dot(traces_part.reshape(seg_dev * rows, samples), table, preferred_el...  67.4 us
    all_to_all x1, blocking collectives, body(): lax.all_to_all(white, 'tm', split_axis=2, concat_axis=0, tiled=True)  55.9 us
    unnamed x37, local copies, waits for them, and re-layouts  35.7 us
    reshape x3, local copies, waits for them, and re-layouts, band(): return flat.reshape(rows, width + 1, extra)[:, 1:rows + 1, :]  28.7 us
    dot_general x4, matrix products, product(): jnp.einsum('sah,sbh->abh', left, right, preferred_element_type=jnp.float32)  24.2 us
    max x1, other arithmetic, whiten(): level = jnp.maximum(smooth, water).reshape(lead + (groups, 1, width))  18.4 us
  transfers between devices with their start and end apart: 3, of which 1 were waited for; matrix products, arithmetic and copies ran while one was open for 15% of the time, Pallas kernels for 0%

profile of v1, /device:TPU:15, one launch (start us, length us, event | category | flops | bytes accessed | tf_op | source)
XLA Modules:
  0.0 495.3 jit_solution(8928700729832364326)
XLA Ops:
  0.0 67.4 %select_convert_fusion.4 = bf16[2048,2048]{1,0:T(8,128)(2,1)S(1)} fusion(s32[2048]{0:T(1024)S(1)} %fusion.71, pred[2048]{0:T(1024)(128)(4,1)S(1)} %fusion.68), kind=kLoop, calls=%fused_computation.15.clone.clone.1 | loop fusion | flops 71303168 | bytes 8398848 | tf_op jit(solution)/shard_map/dot_general | solution.py:88
  67.5 11.0 %fusion.12 = f32[2048,1024]{0,1:T(8,128)} fusion(bf16[1024,2048]{1,0:T(8,128)(2,1)S(1)} %bitcast.137, bf16[2048,2048]{1,0:T(8,128)(2,1)S(1)} %select_convert_fusion.4), kind=kOutput, calls=%fused_computation.21 | convolution fusion | flops 8589934592 | bytes 20971520 | tf_op jit(solution)/shard_map/dot_general | solution.py:88
  78.5 9.7 %copy.36 = f32[1024,2048]{0,1:T(8,128)} copy(f32[1024,2048]{1,0:T(8,128)} %bitcast.127) | data formatting | bytes 16777216 | tf_op jit(solution)/shard_map/dot_general | solution.py:88
  88.2 5.5 %copy.56 = f32[256,8,8,128]{3,2,1,0:T(8,128)S(1)} copy(f32[256,8,8,128]{3,1,2,0:T(8,128)} %bitcast.130) | data formatting | bytes 16777216
  93.7 1.5 fusion.82
  95.2 2.8 copy.37
  97.9 9.1 %copy.38 = f32[8,128,2048]{1,2,0:T(8,128)} copy(f32[8,128,2048]{2,1,0:T(8,128)} %bitcast.128) | data formatting | bytes 16777216 | tf_op jit(solution)/shard_map/reshape;reshape | solution.py:52
  107.1 18.4 %multiply_maximum_fusion = f32[8,128,1024]{1,2,0:T(8,128)} fusion(f32[8,128,1024]{1,2,0:T(8,128)} %bitcast.132, f32[8,128]{1,0:T(8,128)S(1)} %multiply_add_fusion), kind=kLoop, calls=%fused_computation.49 | loop fusion | flops 10485760 | bytes 8392704 | tf_op jit(solution)/shard_map/max | solution.py:59
  125.4 5.0 %fusion.14 = bf16[8,128,2048]{1,2,0:T(8,128)(2,1)} fusion(f32[8,128,2048]{1,2,0:T(8,128)S(1)} %copy-done, f32[8,128,16,64]{1,3,2,0:T(8,128)} %bitcast.133), kind=kLoop, calls=%fused_computation.26 | loop fusion | flops 4194304 | bytes 16777216 | tf_op jit(solution)/shard_map/convert_element_type | solution.py:60
  130.5 4.9 copy.39
  135.4 55.9 %all_to_all.23 = bf16[8,128,2048]{1,0,2:T(8,128)(2,1)S(1)} all-to-all(bf16[8,128,2048]{1,0,2:T(8,128)(2,1)S(1)} %copy.39), channel_id=1, replica_groups=mesh['chan'=8,'tm'=16] {'tm'}, dimensions={2} | all-to-all | bytes 8388608 | tf_op jit(solution)/shard_map/all_to_all | solution.py:104
  191.3 3.2 copy.68
  194.5 2.4 collective-permute-start
  196.9 2.2 collective-permute-start.1
  199.1 92.9 %collective-permute-done.1 = bf16[128]{0:T(256)(128)(2,1)S(1)} collective-permute-done((bf16[128]{0:T(256)(128)(2,1)S(1)}, bf16[128]{0:T(256)(128)(2,1)S(1)}, u32[]{:S(2)}, u32[]{:S(2)}) %collective-permute-start.1) | collective-permute-done | bytes 288 | tf_op jit(solution)/shard_map/ppermute | solution.py:19
  292.9 0.7 slice_bitcast_fusion.16
  293.7 4.2 fusion.40
  297.9 7.9 %add_bitcast_fusion = f32[128,256,64]{0,1,2:T(8,128)} fusion(f32[64,256,128]{2,1,0:T(8,128)S(1)} %fusion.40, bf16[128,128,128]{1,0,2:T(8,128)(2,1)} %bitcast.124, bf16[128,128,128]{1,0,2:T(8,128)(2,1)} %collective-permute-done), kind=kOutput, calls=%fused_computation.31 | convolution fusion | flops 555745280 | bytes 27262976 | tf_op jit(solution)/shard_map/sah,sbh->abh/dot_general | solution.py:71
  305.7 9.3 %copy.57 = f32[8,8,128,256]{3,1,2,0:T(8,128)} copy(f32[8,8,128,256]{2,3,1,0:T(8,128)} %bitcast.135) | data formatting | bytes 16777216
  315.1 7.2 %pad.16 = f32[32896,64]{0,1:T(8,128)} pad(f32[32768,64]{0,1:T(8,128)} %bitcast.126, f32[]{:T(128)} %constant.116.clone.1), padding=0_128x0_0 | pad | bytes 16809988 | tf_op jit(solution)/shard_map/jit(_pad)/pad | solution.py:66
  322.3 14.2 %reshape.180 = f32[128,257,64]{1,0,2:T(8,128)} reshape(f32[32896,64]{0,1:T(8,128)} %pad.16) | data formatting | bytes 16842752 | tf_op jit(solution)/shard_map/reshape | solution.py:67
  336.4 6.5 %slice.73 = f32[128,128,64]{1,0,2:T(8,128)} slice(f32[128,257,64]{1,0,2:T(8,128)} %reshape.180), slice={[0:128], [1:129], [0:64]} | slice | bytes 8388608 | tf_op jit(solution)/shard_map/slice | solution.py:67
  342.9 4.2 fusion.42
  347.2 7.9 %subtract_bitcast_fusion = f32[128,256,64]{0,1,2:T(8,128)} fusion(f32[64,256,128]{2,1,0:T(8,128)S(1)} %fusion.42, bf16[128,128,128]{1,0,2:T(8,128)(2,1)} %bitcast.124, bf16[128,128,128]{1,0,2:T(8,128)(2,1)} %collective-permute-done), kind=kOutput, calls=%fused_computation.30 | convolution fusion | flops 555745280 | bytes 27262976 | tf_op jit(solution)/shard_map/sah,sbh->abh/dot_general | solution.py:71
  355.1 9.2 %copy.58 = f32[8,8,128,256]{3,1,2,0:T(8,128)} copy(f32[8,8,128,256]{2,3,1,0:T(8,128)} %bitcast.134) | data formatting | bytes 16777216
  364.2 7.2 %pad.17 = f32[32896,64]{0,1:T(8,128)} pad(f32[32768,64]{0,1:T(8,128)} %bitcast.125, f32[]{:T(128)} %constant.116.clone.1), padding=0_128x0_0 | pad | bytes 16809988 | tf_op jit(solution)/shard_map/jit(_pad)/pad | solution.py:66
  371.4 14.2 %reshape.182 = f32[128,257,64]{1,0,2:T(8,128)} reshape(f32[32896,64]{0,1:T(8,128)} %pad.17) | data formatting | bytes 16842752 | tf_op jit(solution)/shard_map/reshape | solution.py:67
  385.6 4.7 slice.74
  390.3 1.2 fusion.13
  391.5 0.8 fusion.60
  392.3 0.8 fusion.59
  393.0 0.8 fusion.58
  393.8 0.8 fusion.57
  394.6 0.8 fusion.56
  395.4 0.8 fusion.55
  396.1 0.8 fusion.54
  396.9 0.8 fusion.53
  397.7 0.8 fusion.52
  398.4 0.8 fusion.51
  399.2 0.8 fusion.50
  400.0 0.8 fusion.49
  400.8 0.8 fusion.48
  401.5 0.8 fusion.47
  402.3 0.8 fusion.46
  403.1 0.8 fusion.45
  403.9 6.0 %all-to-all-start.1 = ((bf16[16,8,128,128]{2,1,3,0:T(8,128)(2,1)}), bf16[16,8,128,128]{2,1,3,0:T(8,128)(2,1)}, u32[]{:S(2)}, u32[]{:S(2)}) async-start(bf16[16,8,128,128]{2,1,3,0:T(8,128)(2,1)} %fusion.45), calls=%async_computation.1 | async-start | bytes 8388608 | tf_op jit(solution)/shard_map/all_to_all | solution.py:12
  409.9 71.1 %fusion.90 = bf16[2048,2048,1]{1,0,2:T(8,128)(2,1)} fusion(s32[2048]{0:T(1024)S(1)} %iota_add_fusion, s32[2048]{0:T(1024)S(1)} %copy-done.4, f32[2048]{0:T(1024)S(1)} %select_multiply_fusion, pred[2048]{0:T(1024)(128)(4,1)S(1)} %copy-done.6), kind=kLoop, calls=%fused_computation.19.clone.clone.clone.clone.1 | loop fusion | flops 75497472 | bytes 8415232 | tf_op jit(solution)/shard_map/rif,fl->ril/dot_general | solution.py:109
  481.0 14.0 %fusion.34 = bf16[8,128,2048]{2,1,0:T(8,128)(2,1)} fusion(bf16[8,128,2048]{1,0,2:T(8,128)(2,1)} %bitcast.30, bf16[2048,2048,1]{1,0,2:T(8,128)(2,1)} %fusion.90), kind=kOutput, calls=%fused_computation.55 | convolution fusion | flops 8592031744 | bytes 16777216 | tf_op jit(solution)/shard_map/rif,fl->ril/dot_general | solution.py:109
  (31 shorter events, 1.0 us)
Async XLA Ops:
  0.0 67.5 %copy-start.3 = (s32[2048]{0:T(1024)}, s32[2048]{0:T(1024)S(1)}, u32[]{:S(2)}) copy-start(s32[2048]{0:T(1024)S(1)} %fusion.71) | copy-start | bytes 24580
  0.0 67.5 %copy-start.5 = (pred[2048]{0:T(1024)(128)(4,1)}, pred[2048]{0:T(1024)(128)(4,1)S(1)}, u32[]{:S(2)}) copy-start(pred[2048]{0:T(1024)(128)(4,1)S(1)} %fusion.68) | copy-start | bytes 6148
  0.0 67.5 %copy-start.7 = (bf16[8,128,2048]{2,1,0:T(8,128)(2,1)S(1)}, bf16[8,128,2048]{2,1,0:T(8,128)(2,1)}, u32[]{:S(2)}) copy-start(bf16[8,128,2048]{2,1,0:T(8,128)(2,1)} %param.2) | copy-start | bytes 12582916
  107.1 18.4 %copy-start = (f32[8,128,2048]{1,2,0:T(8,128)S(1)}, f32[8,128,2048]{1,2,0:T(8,128)}, u32[]{:S(2)}) copy-start(f32[8,128,2048]{1,2,0:T(8,128)} %copy.38) | copy-start | bytes 25165828
  191.3 5.7 %copy-start.8 = (s32[128]{0:T(128)S(1)}, s32[128]{0:T(128)}, u32[]{:S(2)}) copy-start(s32[128]{0:T(128)} %param.3) | copy-start | bytes 1540
  194.5 99.2 %collective-permute-start = (bf16[128,128,128]{1,0,2:T(8,128)(2,1)}, bf16[128,128,128]{1,0,2:T(8,128)(2,1)}, u32[]{:S(2)}, u32[]{:S(2)}) collective-permute-start(bf16[128,128,128]{1,0,2:T(8,128)(2,1)} %bitcast.124), channel_id=1, source_target_pairs={{16,0},{32,16},{48,32},{64,48},{80,64},{96,80},{112,96},{17,1},{33... | collective-permute-start | bytes 12582920 | tf_op jit(solution)/shard_map/ppermute | solution.py:19
  196.9 95.1 %collective-permute-start.1 = (bf16[128]{0:T(256)(128)(2,1)S(1)}, bf16[128]{0:T(256)(128)(2,1)S(1)}, u32[]{:S(2)}, u32[]{:S(2)}) collective-permute-start(bf16[128]{0:T(256)(128)(2,1)S(1)} %get-tuple-element.8), channel_id=1, source_target_pairs={{16,0},{32,16},{48,32},{64,48},{80,64},{96,80},{112,96},{17,1},{33... | collective-permute-start | bytes 776 | tf_op jit(solution)/shard_map/ppermute | solution.py:19
  385.6 4.7 copy-start.1
  385.6 4.7 copy-start.2
  403.9 6.0 %copy-start.4 = (s32[2048]{0:T(1024)S(1)}, s32[2048]{0:T(1024)}, u32[]{:S(2)}) copy-start(s32[2048]{0:T(1024)} %copy-done.3) | copy-start | bytes 24580
  403.9 6.0 %copy-start.6 = (pred[2048]{0:T(1024)(128)(4,1)S(1)}, pred[2048]{0:T(1024)(128)(4,1)}, u32[]{:S(2)}) copy-start(pred[2048]{0:T(1024)(128)(4,1)} %copy-done.5) | copy-start | bytes 6148
  403.9 77.1 %all-to-all-start.1 = ((bf16[16,8,128,128]{2,1,3,0:T(8,128)(2,1)}), bf16[16,8,128,128]{2,1,3,0:T(8,128)(2,1)}, u32[]{:S(2)}, u32[]{:S(2)}) async-start(bf16[16,8,128,128]{2,1,3,0:T(8,128)(2,1)} %fusion.45), calls=%async_computation.1 | async-start | bytes 8388608 | tf_op jit(solution)/shard_map/all_to_all | solution.py:12
